TPU v7x, 512 devices: a whole 4x8x8 slice. The times are simulated.
512 devices in a mesh: pipe: 32 (over y, z_lo), seq: 16 (over z_hi, x, core).
Axes of the slice: x: 4, y: 8, z: 8 (z_hi: 2, z_lo: 4; z = z_hi * 4 + z_lo), core: 2. Of those that a mesh axis runs over, the one named last changes fastest.
Arguments:
- x_first: bfloat16 [4096, 2560], P(('pipe', 'seq')), may hold values from -6 to 6
- x_second: bfloat16 [4096, 2560], P(('pipe', 'seq')), may hold values from -6 to 6
- stale_kv: bfloat16 [2, 4096, 2048], P(None, 'pipe', 'seq'), may hold values from -6 to 6
- w_qkv: bfloat16 [3, 2560, 2048], P(None, None, 'seq'), may hold values from -0.125 to 0.125
- w_out: bfloat16 [2048, 2560], P('seq'), may hold values from -0.125 to 0.125
- q_gain: float32 [2048], P('seq'), may hold values from 0.4 to 5
- k_gain: float32 [2048], P('seq'), may hold values from 0.4 to 5
- layout: int32 [32, 16], replicated, may hold values from 0 to 31, as said below
- counts: int32 [32], replicated, may hold values from 1 to 16, as said below
- slot_block: int32 [32], replicated, may hold values from 0 to 31, each once
Outputs:
- out_first: bfloat16 [4096, 2560], P(('pipe', 'seq'))
- out_second: bfloat16 [4096, 2560], P(('pipe', 'seq'))
Inputs may be any that keep to these rules, and one draw needn't show every extreme that they name: `layout`: entries of a row are distinct sequence blocks and the first entry of row b is b itself. `counts`: some block reads 16 entries. `slot_block`: each block once.
All inputs are finite; a program needn't handle non-finite values.
Results may differ from a plain program's by a relative error of at most 0.019.
Values may be sent and summed in bfloat16 or wider, within the bound.
No kernel may reach another device: no remote copies, remote signals or barrier semaphores. Data moves between devices by JAX's collectives and lax.ppermute only.
A program may use at most 64 MiB of HBM per device.

v0:
```python
import math
import jax
import jax.numpy as jnp
import numpy as np
from jax import lax
from jax.sharding import Mesh
from jax.sharding import PartitionSpec as P

HS = 64
BLOCK = 128
BPM = 1
HIGH = lax.Precision.HIGHEST
NEG = -1e30
PIPE_PARTS = (("y", 8), ("zl", 4))
SEQ_PARTS = (("zh", 2), ("x", 4), ("c", 2))
PIPE = tuple((n for n, _ in PIPE_PARTS))
SEQ = tuple((n for n, _ in SEQ_PARTS))


def slot_mask(layout, counts, slot_block):
    total = layout.shape[0]
    width = layout.shape[1]
    blocks = jnp.arange(total, dtype=jnp.int32)
    valid = jnp.arange(width, dtype=jnp.int32)[None, :] < counts[:, None]
    member = jnp.sum(
        ((layout[:, :, None] == blocks[None, None, :]) & valid[:, :, None]).astype(jnp.float32),
        axis=1,
    )
    placed = (slot_block[:, None] == blocks[None, :]).astype(jnp.float32)
    linked = jnp.dot(jnp.dot(placed, member, precision=HIGH), placed.T, precision=HIGH)
    return linked > 0.5


def normalize(raw, gain, size):
    count = raw.shape[0]
    grid = raw.reshape(count, -1, size)
    factor = lax.rsqrt(jnp.mean(grid * grid, axis=2, keepdims=True) + 1e-06)
    return (grid * factor).reshape(count, -1) * gain[None, :]


def partial_attend(query, keys, values, allowed, scale):
    heads = query.shape[1]
    qrows = query.shape[0]
    krows = keys.shape[0]
    scores = jnp.einsum("qhd,khd->hqk", query, keys, preferred_element_type=jnp.float32) * scale
    grid = scores.reshape(heads, qrows // BLOCK, BLOCK, krows // BLOCK, BLOCK)
    keep = allowed[None, :, None, :, None]
    grid = jnp.where(keep, grid, NEG)
    top = jnp.max(grid, axis=(3, 4))
    weights = jnp.where(keep, jnp.exp(grid - top[:, :, :, None, None]), 0.0)
    total = jnp.sum(weights, axis=(3, 4))
    weights = weights.reshape(heads, qrows, krows)
    summed = jnp.einsum("hqk,khd->qhd", weights, values.astype(jnp.float32), precision=HIGH)
    return (top.reshape(heads, qrows), total.reshape(heads, qrows), summed)


def merge_parts(first, second):
    top_a, total_a, summed_a = first
    top_b, total_b, summed_b = second
    best = jnp.maximum(top_a, top_b)
    keep_a = jnp.exp(top_a - best)
    keep_b = jnp.exp(top_b - best)
    merged = summed_a * keep_a.T[:, :, None] + summed_b * keep_b.T[:, :, None]
    return (best, total_a * keep_a + total_b * keep_b, merged)


def gather_pipe(piece):
    for name in reversed(PIPE):
        piece = lax.all_gather(piece, name, axis=0, tiled=True)
    return piece


def on_device(
    x_first, x_second, stale_kv, w_qkv, w_out, q_gain, k_gain, layout, counts, slot_block
):
    me = lax.axis_index(PIPE)
    n_seq = math.prod((s for _, s in SEQ_PARTS))
    tokens = BPM * BLOCK
    heads = w_qkv.shape[2] // HS
    width = heads * HS
    scale = 1.0 / math.sqrt(HS)
    linked = slot_mask(layout, counts, slot_block)
    total_blocks = linked.shape[0]
    block_ids = jnp.arange(total_blocks, dtype=jnp.int32)
    batch_of = block_ids // BPM
    mine = lax.dynamic_slice_in_dim(linked, me * BPM, BPM, 0)
    own = lax.dynamic_slice_in_dim(mine, me * BPM, BPM, 1)
    remote = mine & (batch_of != me)[None, :]
    xs = lax.all_gather(jnp.stack([x_first, x_second]), SEQ, axis=1, tiled=True)

    def project(x):
        raw = jnp.einsum("rd,cdh->crh", x, w_qkv, preferred_element_type=jnp.float32)
        query = normalize(raw[0], q_gain, HS).astype(jnp.bfloat16)
        keys = normalize(raw[1], k_gain, HS).astype(jnp.bfloat16)
        values = raw[2].astype(jnp.bfloat16)
        return (query, keys, values)

    q1, k1, v1 = project(xs[0])
    q2, k2, v2 = project(xs[1])
    kv = jnp.stack([stale_kv[0], stale_kv[1], k1, v1])[None]
    gathered = gather_pipe(kv)
    count = gathered.shape[0] * tokens

    def attend(query, keys, values, piece_k, piece_v):
        query_h = query.reshape(tokens, heads, HS)
        start_part = partial_attend(
            query_h, keys.reshape(tokens, heads, HS), values.reshape(tokens, heads, HS), own, scale
        )
        fresh = partial_attend(
            query_h,
            piece_k.reshape(count, heads, HS),
            piece_v.reshape(count, heads, HS),
            remote,
            scale,
        )
        best, denom_h, numer = merge_parts(start_part, fresh)
        denom = denom_h.T
        attn = (numer / denom[:, :, None]).reshape(tokens, width).astype(jnp.bfloat16)
        return jnp.dot(attn, w_out, preferred_element_type=jnp.float32).astype(jnp.bfloat16)

    part1 = attend(q1, k1, v1, gathered[:, 0], gathered[:, 1])
    part2 = attend(q2, k2, v2, gathered[:, 2], gathered[:, 3])
    parts = jnp.stack([part1, part2])
    sent = lax.all_to_all(parts.reshape(2, n_seq, tokens // n_seq, -1), SEQ, 1, 1, tiled=False)
    out = jnp.sum(sent.astype(jnp.float32), axis=1).astype(jnp.bfloat16)
    return (out[0], out[1])


def solution(mesh):
    names = PIPE_PARTS + SEQ_PARTS
    fine = Mesh(
        np.asarray(mesh.devices).reshape([s for _, s in names]), tuple((n for n, _ in names))
    )
    rows = P(PIPE + SEQ, None)
    placed = (
        rows,
        rows,
        P(None, PIPE, SEQ),
        P(None, None, SEQ),
        P(SEQ, None),
        P(SEQ),
        P(SEQ),
        P(),
        P(),
        P(),
    )
    return jax.shard_map(
        on_device, mesh=fine, in_specs=placed, out_specs=(rows, rows), check_vma=False
    )
```

profile of v0, /device:TPU:64, one launch (start us, length us, event | category | flops | bytes accessed | tf_op | source)
XLA Modules:
  0.0 232.4 jit_solution(3354113923606738813)
XLA Ops:
  7.2 0.0 copy-start
  7.2 0.0 copy-start.5
  7.2 0.0 copy-start.3
  7.2 0.0 all-gather.4.cloned.1.call-start
  7.2 1.5 pad_maximum_fusion.2
  8.7 0.0 all-gather.4.cloned.1.call-update
  8.8 0.0 copy-start.7
  8.8 0.0 copy-start.4
  8.8 0.0 copy-start.6
  8.8 0.0 copy-start.8
  8.8 0.0 all-gather.6.cloned.1.call-start
  8.9 2.7 %copy.33 = bf16[3,2560,128]{1,2,0:T(8,128)(2,1)S(1)} copy(bf16[3,2560,128]{2,1,0:T(8,128)(2,1)} %param.13) | data formatting | bytes 3932160 | tf_op args[3]
  11.5 65.3 %all-gather.4.cloned.1.call-done = bf16[2,128,2560]{2,1,0:T(8,128)(2,1)} async-done(((bf16[2,8,2560]{2,1,0:T(8,128)(2,1)}), bf16[2,128,2560]{2,1,0:T(8,128)(2,1)}) %all-gather.4.cloned.1.call-update) | async-done | bytes 1310736 | tf_op jit(solution)/shard_map/all_gather | solution.py:89
  76.8 1.7 fusion.29
  78.6 0.1 copy.37
  78.8 0.0 copy-done.5
  78.8 0.1 fusion.64
  78.9 0.1 copy.36
  79.0 0.0 copy-done.3
  79.0 15.3 %all-gather = bf16[16,128,128]{2,1,0:T(8,128)(2,1)} all-gather(bf16[4,128,128]{2,1,0:T(8,128)(2,1)S(1)} %pad_maximum_fusion.1), channel_id=2, replica_groups=mesh['y'=8,'zl'=4,'zh'=2,'x'=4,'c'=2] {'zl'}, dimensions={0}, use_global_device_ids=true | all-gather | bytes 655360 | tf_op jit(solution)/shard_map/all_gather | solution.py:69
  94.4 0.0 all-gather.6.cloned.1.call-update
  94.4 0.1 mul.187
  94.5 0.0 copy-done.7
  94.5 0.1 mul.181
  94.6 0.0 copy-done.4
  94.6 0.1 copy.34
  94.7 0.0 copy-done.6
  94.7 0.1 iota_compare_fusion.1
  94.7 0.2 convert_reduce_fusion
  95.0 0.0 copy-done.8
  95.0 0.2 fusion.45
  95.2 0.2 convolution_compare_fusion
  95.4 0.6 dynamic_slice.6
  96.0 0.1 broadcast_bitcast_fusion
  96.1 1.7 fusion.28
  98.0 0.9 fusion.68
  98.9 0.7 fusion.31
  99.6 0.9 fusion.67
  100.6 0.7 fusion.32
  101.3 48.8 %all-gather.6.cloned.1.call-done = bf16[32,4,128,128]{3,2,1,0:T(8,128)(2,1)} async-done(((bf16[4,4,128,128]{3,2,1,0:T(8,128)(2,1)}), bf16[32,4,128,128]{3,2,1,0:T(8,128)(2,1)}) %all-gather.6.cloned.1.call-update) | async-done | bytes 4194320 | tf_op jit(solution)/shard_map/all_gather | solution.py:69
  150.1 4.0 %fusion.62 = (bf16[32,1,128,128]{3,2,1,0:T(8,128)(2,1)}, bf16[32,1,128,128]{3,2,1,0:T(8,128)(2,1)S(1)}, bf16[32,1,128,128]{3,2,1,0:T(8,128)(2,1)}, bf16[32,1,128,128]{3,2,1,0:T(8,128)(2,1)}) fusion(bf16[32,4,128,128]{3,2,1,0:T(8,128)(2,1)} %all-gather.6.cloned.1.call-done), kind=kLoop, calls=%fused_computation.107 | loop fusion | bytes 8388608 | tf_op jit(solution)/shard_map/slice | solution.py:121
  154.1 1.9 copy.39
  156.0 1.3 reshape_squeeze.27
  157.3 1.0 copy.43
  158.3 1.3 reshape_squeeze.31
  159.6 1.9 copy.42
  161.5 0.5 reshape_squeeze.30
  162.0 2.7 %copy.38 = bf16[32,1,128,128]{2,0,3,1:T(8,128)(2,1)} copy(bf16[32,1,128,128]{3,2,1,0:T(8,128)(2,1)} %get-tuple-element.13) | data formatting | bytes 2097152 | tf_op jit(solution)/shard_map/slice | solution.py:121
  164.7 1.7 reshape_squeeze.26
  166.4 0.9 fusion.66
  167.3 0.9 fusion.65
  168.3 1.6 fusion.4
  170.0 0.0 copy-done.2
  170.0 3.1 %fusion.24 = f32[128,2,64]{0,2,1:T(8,128)S(1)} fusion(bf16[4096,2,64]{0,2,1:T(8,128)(2,1)S(1)} %copy-done.2, f32[2,128,4096]{2,1,0:T(8,128)S(1)} %get-tuple-element.23, f32[2,128]{1,0:T(2,128)S(1)} %get-tuple-element.22, pred[4096]{0:T(1024)(128)(4,1)S(1)} %broadcast_bitcast_fusion, f32[128,2]{0,1:T(2,128)S(1)} %get-tuple-element.29), kind=kOutput, calls=%fused_computation.35 | convolution fusion | flops 807419904 | bytes 5314560 | tf_op jit(solution)/shard_map/hqk,khd->qhd/dot_general | solution.py:53
  173.1 0.0 copy-done.1
  173.1 3.1 %fusion.25 = f32[128,2,64]{0,2,1:T(8,128)S(1)} fusion(bf16[4096,2,64]{0,2,1:T(8,128)(2,1)S(1)} %copy-done.1, f32[2,128,4096]{2,1,0:T(8,128)S(1)} %get-tuple-element.21, f32[2,128]{1,0:T(2,128)S(1)} %get-tuple-element.20, pred[4096]{0:T(1024)(128)(4,1)S(1)} %broadcast_bitcast_fusion, f32[128,2]{0,1:T(2,128)S(1)} %get-tuple-element.9), kind=kOutput, calls=%fused_computation.36 | convolution fusion | flops 807419904 | bytes 5314560 | tf_op jit(solution)/shard_map/hqk,khd->qhd/dot_general | solution.py:53
  176.2 0.9 fusion.26
  177.1 0.4 fusion.3
  177.4 0.9 fusion.27
  178.3 0.3 fusion.2
  178.6 0.1 pad_maximum_fusion
  178.8 46.0 %all_to_all.5 = bf16[2,16,8,2560]{3,2,0,1:T(8,128)(2,1)S(1)} all-to-all(bf16[2,16,8,2560]{3,2,0,1:T(8,128)(2,1)S(1)} %pad_maximum_fusion), channel_id=1, replica_groups=mesh['y'=8,'zl'=4,'zh'=2,'x'=4,'c'=2] {'zh','x','c'}, dimensions={1} | all-to-all | bytes 2621440 | tf_op jit(solution)/shard_map/all_to_all | solution.py:124
  224.8 0.2 reduce_sum.114
  225.0 0.6 slice_bitcast_fusion.4
  (18 shorter events, 0.2 us)
Async XLA Ops:
  7.2 169.9 %copy-start = (bf16[128,2560]{1,0:T(8,128)(2,1)S(1)}, bf16[128,2560]{1,0:T(8,128)(2,1)}, u32[]{:S(2)}) copy-start(bf16[128,2560]{1,0:T(8,128)(2,1)} %param.14) | copy-start | bytes 1966084
  7.2 71.6 %copy-start.5 = (f32[128]{0:T(128)S(1)}, f32[128]{0:T(128)}, u32[]{:S(2)}) copy-start(f32[128]{0:T(128)} %param.16) | copy-start | bytes 1540
  7.2 71.8 %copy-start.3 = (bf16[2,128,128]{2,1,0:T(8,128)(2,1)S(1)}, bf16[2,128,128]{2,1,0:T(8,128)(2,1)}, u32[]{:S(2)}) copy-start(bf16[2,128,128]{2,1,0:T(8,128)(2,1)} %param.12) | copy-start | bytes 196612
  7.2 69.6 %all-gather.4.cloned.1.call-start = ((), (), s32[]{:S(2)}) async-start(), calls=%async_computation.1 | async-start | bytes 1392640 | tf_op jit(solution)/shard_map/all_gather | solution.py:89
  8.8 85.7 %copy-start.7 = (f32[128]{0:T(128)S(1)}, f32[128]{0:T(128)}, u32[]{:S(2)}) copy-start(f32[128]{0:T(128)} %param.15) | copy-start | bytes 1540
  8.8 85.8 %copy-start.4 = (s32[32,16]{0,1:T(8,128)S(1)}, s32[32,16]{0,1:T(8,128)}, u32[]{:S(2)}) copy-start(s32[32,16]{0,1:T(8,128)} %param.17) | copy-start | bytes 6148
  8.8 85.9 %copy-start.6 = (s32[32]{0:T(128)S(1)}, s32[32]{0:T(128)}, u32[]{:S(2)}) copy-start(s32[32]{0:T(128)} %param.18) | copy-start | bytes 388
  8.8 86.2 %copy-start.8 = (s32[32]{0:T(128)S(1)}, s32[32]{0:T(128)}, u32[]{:S(2)}) copy-start(s32[32]{0:T(128)} %param.19) | copy-start | bytes 388
  8.8 141.3 %all-gather.6.cloned.1.call-start = ((), (), s32[]{:S(2)}) async-start(), calls=%async_computation.2 | async-start | bytes 4718592 | tf_op jit(solution)/shard_map/all_gather | solution.py:69
  168.3 1.7 copy-start.2
  169.9 3.1 %copy-start.1 = (bf16[4096,2,64]{0,2,1:T(8,128)(2,1)S(1)}, bf16[4096,2,64]{0,2,1:T(8,128)(2,1)}, u32[]{:S(2)}) copy-start(bf16[4096,2,64]{0,2,1:T(8,128)(2,1)} %reshape_squeeze.31) | copy-start | bytes 3145732
Sparse Core Ops, SparseCore 0:
  11.4 65.4 all-gather.3
  94.5 55.5 all-gather.5
where the time goes:
time: 233 us; the launch traced here: 232 us
  waiting for transfers between devices  114 us (49%)
  blocking collectives  61.4 us (26%)
  local copies, waits for them, and re-layouts  20.8 us (9%)
  matrix products  16.3 us (7%)
  between operations  14.4 us (6%)
  other arithmetic  5.38 us (2%)
    all_gather x1, waiting for transfers between devices, on_device(): xs = lax.all_gather(jnp.stack([x_first, x_second]), SEQ, axis=1, tiled=True)  65.3 us
    all_gather x1, waiting for transfers between devices, gather_pipe(): piece = lax.all_gather(piece, name, axis=0, tiled=True)  48.8 us
    all_to_all x1, blocking collectives, on_device(): lax.all_to_all(parts.reshape(2, n_seq, tokens // n_seq, -1), SEQ, 1, 1, t...  46 us
    all_gather x1, blocking collectives, gather_pipe(): piece = lax.all_gather(piece, name, axis=0, tiled=True)  15.3 us
    slice x3, local copies, waits for them, and re-layouts, on_device(): part1 = attend(q1, k1, v1, gathered[:, 0], gathered[:, 1])  8.57 us
    dot_general x4, matrix products, partial_attend(): jnp.einsum('hqk,khd->qhd', weights, values.astype(jnp.float32), precision...  7.93 us
  transfers between devices with their start and end apart: 2, of which 2 were waited for; matrix products, arithmetic and copies ran while one was open for 4% of the time, Pallas kernels for 0%

commit v1 on v0

--- a/solution.py
+++ b/solution.py
@@ -86,7 +86,10 @@
     mine = lax.dynamic_slice_in_dim(linked, me * BPM, BPM, 0)
     own = lax.dynamic_slice_in_dim(mine, me * BPM, BPM, 1)
     remote = mine & (batch_of != me)[None, :]
-    xs = lax.all_gather(jnp.stack([x_first, x_second]), SEQ, axis=1, tiled=True)
+    xs = jnp.concatenate(
+        lax.all_to_all(jnp.stack([jnp.stack([x_first, x_second])] * lax.axis_size(SEQ)), SEQ, 0, 0),
+        axis=1,
+    )
 
     def project(x):
         raw = jnp.einsum("rd,cdh->crh", x, w_qkv, preferred_element_type=jnp.float32)

time: 233 us -> 214 us (0.918)
  waiting for transfers between devices: 114 us -> 84 us
  starting transfers between devices: 0.08 us -> 12 us
    all_gather x1 -> x0, waiting for transfers between devices: 65.3 us -> none  [on_device(): xs = lax.all_gather(jnp.stack([x_first, x_second]), SEQ, axis=1, tiled=True)]
    all_to_all x0 -> x1, waiting for transfers between devices: none -> 34.5 us  [on_device(): lax.all_to_all(jnp.stack([jnp.stack([x_first, x_second])] * lax.axis_size...]
    all_to_all x0 -> x1, starting transfers between devices: none -> 12 us  [on_device(): lax.all_to_all(jnp.stack([jnp.stack([x_first, x_second])] * lax.axis_size...]
where the time goes in v1:
time: 214 us; the launch traced here: 213 us
  waiting for transfers between devices  84 us (39%)
  blocking collectives  59.7 us (28%)
  local copies, waits for them, and re-layouts  21.9 us (10%)
  matrix products  16.3 us (8%)
  between operations  14.4 us (7%)
  starting transfers between devices  12 us (6%)
  other arithmetic  4.77 us (2%)
    all_gather x1, waiting for transfers between devices, gather_pipe(): piece = lax.all_gather(piece, name, axis=0, tiled=True)  49.5 us
    all_to_all x1, blocking collectives, on_device(): lax.all_to_all(parts.reshape(2, n_seq, tokens // n_seq, -1), SEQ, 1, 1, t...  46 us
    all_to_all x1, waiting for transfers between devices, on_device(): lax.all_to_all(jnp.stack([jnp.stack([x_first, x_second])] * lax.axis_size...  34.5 us
    all_gather x1, blocking collectives, gather_pipe(): piece = lax.all_gather(piece, name, axis=0, tiled=True)  13.7 us
    all_to_all x1, starting transfers between devices, on_device(): lax.all_to_all(jnp.stack([jnp.stack([x_first, x_second])] * lax.axis_size...  12 us
    slice x3, local copies, waits for them, and re-layouts, on_device(): part1 = attend(q1, k1, v1, gathered[:, 0], gathered[:, 1])  8.57 us
    dot_general x4, matrix products, partial_attend(): jnp.einsum('hqk,khd->qhd', weights, values.astype(jnp.float32), precision...  7.93 us
  transfers between devices with their start and end apart: 2, of which 2 were waited for; matrix products, arithmetic and copies ran while one was open for 4% of the time, Pallas kernels for 0%

profile of v1, /device:TPU:64, one launch (start us, length us, event | category | flops | bytes accessed | tf_op | source)
XLA Modules:
  0.0 213.2 jit_solution(6781140944320013016)
XLA Ops:
  7.2 0.0 copy-start
  7.2 0.9 pad_maximum_fusion.2
  8.1 1.2 stack.20
  9.2 12.0 %all-to-all-start = ((bf16[16,2,8,2560]{3,2,1,0:T(8,128)(2,1)}), bf16[16,2,8,2560]{3,2,1,0:T(8,128)(2,1)}, u32[]{:S(2)}, u32[]{:S(2)}) async-start(bf16[16,2,8,2560]{3,2,1,0:T(8,128)(2,1)} %stack.20), calls=%async_computation | async-start | bytes 2621440 | tf_op jit(solution)/shard_map/all_to_all | solution.py:90
  21.2 0.0 copy-start.5
  21.3 0.0 copy-start.3
  21.3 0.0 copy-start.7
  21.3 0.0 copy-start.4
  21.3 0.0 copy-start.6
  21.3 0.0 copy-start.8
  21.3 0.0 all-gather.3.cloned.1.call-start
  21.4 2.7 %copy.33 = bf16[3,2560,128]{1,2,0:T(8,128)(2,1)S(1)} copy(bf16[3,2560,128]{2,1,0:T(8,128)(2,1)} %param.13) | data formatting | bytes 3932160 | tf_op args[3]
  24.1 34.5 %all-to-all-done = bf16[16,2,8,2560]{3,2,1,0:T(8,128)(2,1)} async-done(((bf16[16,2,8,2560]{3,2,1,0:T(8,128)(2,1)}), bf16[16,2,8,2560]{3,2,1,0:T(8,128)(2,1)}, u32[]{:S(2)}, u32[]{:S(2)}) %all-to-all-start) | async-done | bytes 1310752 | tf_op jit(solution)/shard_map/all_to_all | solution.py:90
  58.5 1.7 fusion.29
  60.3 0.1 copy.37
  60.5 0.0 copy-done.5
  60.5 0.1 fusion.64
  60.6 0.1 copy.36
  60.7 0.0 copy-done.3
  60.7 13.7 %all-gather = bf16[16,128,128]{2,1,0:T(8,128)(2,1)} all-gather(bf16[4,128,128]{2,1,0:T(8,128)(2,1)S(1)} %pad_maximum_fusion.1), channel_id=2, replica_groups=mesh['y'=8,'zl'=4,'zh'=2,'x'=4,'c'=2] {'zl'}, dimensions={0}, use_global_device_ids=true | all-gather | bytes 655360 | tf_op jit(solution)/shard_map/all_gather | solution.py:69
  74.4 0.0 all-gather.3.cloned.1.call-update
  74.5 0.1 mul.187
  74.6 0.0 copy-done.7
  74.6 0.1 mul.181
  74.6 0.0 copy-done.4
  74.6 0.1 copy.34
  74.7 0.0 copy-done.6
  74.7 0.1 iota_compare_fusion.1
  74.8 0.2 convert_reduce_fusion
  75.0 0.0 copy-done.8
  75.0 0.2 fusion.45
  75.2 0.2 convolution_compare_fusion
  75.4 0.6 dynamic_slice.6
  76.1 0.1 broadcast_bitcast_fusion
  76.1 1.7 fusion.28
  78.0 0.9 fusion.68
  79.0 0.7 fusion.31
  79.7 0.9 fusion.67
  80.6 0.7 fusion.32
  81.3 49.5 %all-gather.3.cloned.1.call-done = bf16[32,4,128,128]{3,2,1,0:T(8,128)(2,1)} async-done(((bf16[4,4,128,128]{3,2,1,0:T(8,128)(2,1)}), bf16[32,4,128,128]{3,2,1,0:T(8,128)(2,1)}) %all-gather.3.cloned.1.call-update) | async-done | bytes 4194320 | tf_op jit(solution)/shard_map/all_gather | solution.py:69
  130.8 4.0 %fusion.62 = (bf16[32,1,128,128]{3,2,1,0:T(8,128)(2,1)}, bf16[32,1,128,128]{3,2,1,0:T(8,128)(2,1)S(1)}, bf16[32,1,128,128]{3,2,1,0:T(8,128)(2,1)}, bf16[32,1,128,128]{3,2,1,0:T(8,128)(2,1)}) fusion(bf16[32,4,128,128]{3,2,1,0:T(8,128)(2,1)} %all-gather.3.cloned.1.call-done), kind=kLoop, calls=%fused_computation.107 | loop fusion | bytes 8388608 | tf_op jit(solution)/shard_map/slice | solution.py:124
  134.8 1.9 copy.39
  136.7 1.3 reshape_squeeze.27
  138.0 1.0 copy.43
  139.0 1.3 reshape_squeeze.31
  140.3 1.9 copy.42
  142.2 0.5 reshape_squeeze.30
  142.7 2.7 %copy.38 = bf16[32,1,128,128]{2,0,3,1:T(8,128)(2,1)} copy(bf16[32,1,128,128]{3,2,1,0:T(8,128)(2,1)} %get-tuple-element.13) | data formatting | bytes 2097152 | tf_op jit(solution)/shard_map/slice | solution.py:124
  145.4 1.7 reshape_squeeze.26
  147.1 0.9 fusion.66
  148.0 0.9 fusion.65
  149.0 1.6 fusion.4
  150.7 0.0 copy-done.2
  150.7 3.1 %fusion.24 = f32[128,2,64]{0,2,1:T(8,128)S(1)} fusion(bf16[4096,2,64]{0,2,1:T(8,128)(2,1)S(1)} %copy-done.2, f32[2,128,4096]{2,1,0:T(8,128)S(1)} %get-tuple-element.23, f32[2,128]{1,0:T(2,128)S(1)} %get-tuple-element.22, pred[4096]{0:T(1024)(128)(4,1)S(1)} %broadcast_bitcast_fusion, f32[128,2]{0,1:T(2,128)S(1)} %get-tuple-element.29), kind=kOutput, calls=%fused_computation.35 | convolution fusion | flops 807419904 | bytes 5314560 | tf_op jit(solution)/shard_map/hqk,khd->qhd/dot_general | solution.py:53
  153.8 0.0 copy-done.1
  153.8 3.1 %fusion.25 = f32[128,2,64]{0,2,1:T(8,128)S(1)} fusion(bf16[4096,2,64]{0,2,1:T(8,128)(2,1)S(1)} %copy-done.1, f32[2,128,4096]{2,1,0:T(8,128)S(1)} %get-tuple-element.21, f32[2,128]{1,0:T(2,128)S(1)} %get-tuple-element.20, pred[4096]{0:T(1024)(128)(4,1)S(1)} %broadcast_bitcast_fusion, f32[128,2]{0,1:T(2,128)S(1)} %get-tuple-element.9), kind=kOutput, calls=%fused_computation.36 | convolution fusion | flops 807419904 | bytes 5314560 | tf_op jit(solution)/shard_map/hqk,khd->qhd/dot_general | solution.py:53
  156.9 0.9 fusion.26
  157.8 0.4 fusion.3
  158.1 0.9 fusion.27
  159.0 0.3 fusion.2
  159.4 0.1 pad_maximum_fusion
  159.5 46.0 %all_to_all.10 = bf16[2,16,8,2560]{3,2,0,1:T(8,128)(2,1)S(1)} all-to-all(bf16[2,16,8,2560]{3,2,0,1:T(8,128)(2,1)S(1)} %pad_maximum_fusion), channel_id=1, replica_groups=mesh['y'=8,'zl'=4,'zh'=2,'x'=4,'c'=2] {'zh','x','c'}, dimensions={1} | all-to-all | bytes 2621440 | tf_op jit(solution)/shard_map/all_to_all | solution.py:127
  205.5 0.2 reduce_sum.114
  205.7 0.6 slice_bitcast_fusion.4
  (18 shorter events, 0.2 us)
Async XLA Ops:
  7.2 150.6 %copy-start = (bf16[128,2560]{1,0:T(8,128)(2,1)S(1)}, bf16[128,2560]{1,0:T(8,128)(2,1)}, u32[]{:S(2)}) copy-start(bf16[128,2560]{1,0:T(8,128)(2,1)} %param.14) | copy-start | bytes 1966084
  9.2 49.3 %all-to-all-start = ((bf16[16,2,8,2560]{3,2,1,0:T(8,128)(2,1)}), bf16[16,2,8,2560]{3,2,1,0:T(8,128)(2,1)}, u32[]{:S(2)}, u32[]{:S(2)}) async-start(bf16[16,2,8,2560]{3,2,1,0:T(8,128)(2,1)} %stack.20), calls=%async_computation | async-start | bytes 2621440 | tf_op jit(solution)/shard_map/all_to_all | solution.py:90
  21.2 39.2 %copy-start.5 = (f32[128]{0:T(128)S(1)}, f32[128]{0:T(128)}, u32[]{:S(2)}) copy-start(f32[128]{0:T(128)} %param.16) | copy-start | bytes 1540
  21.3 39.4 %copy-start.3 = (bf16[2,128,128]{2,1,0:T(8,128)(2,1)S(1)}, bf16[2,128,128]{2,1,0:T(8,128)(2,1)}, u32[]{:S(2)}) copy-start(bf16[2,128,128]{2,1,0:T(8,128)(2,1)} %param.12) | copy-start | bytes 196612
  21.3 53.3 %copy-start.7 = (f32[128]{0:T(128)S(1)}, f32[128]{0:T(128)}, u32[]{:S(2)}) copy-start(f32[128]{0:T(128)} %param.15) | copy-start | bytes 1540
  21.3 53.4 %copy-start.4 = (s32[32,16]{0,1:T(8,128)S(1)}, s32[32,16]{0,1:T(8,128)}, u32[]{:S(2)}) copy-start(s32[32,16]{0,1:T(8,128)} %param.17) | copy-start | bytes 6148
  21.3 53.4 %copy-start.6 = (s32[32]{0:T(128)S(1)}, s32[32]{0:T(128)}, u32[]{:S(2)}) copy-start(s32[32]{0:T(128)} %param.18) | copy-start | bytes 388
  21.3 53.7 %copy-start.8 = (s32[32]{0:T(128)S(1)}, s32[32]{0:T(128)}, u32[]{:S(2)}) copy-start(s32[32]{0:T(128)} %param.19) | copy-start | bytes 388
  21.3 109.5 %all-gather.3.cloned.1.call-start = ((), (), s32[]{:S(2)}) async-start(), calls=%async_computation.2 | async-start | bytes 4718592 | tf_op jit(solution)/shard_map/all_gather | solution.py:69
  149.0 1.7 copy-start.2
  150.6 3.1 %copy-start.1 = (bf16[4096,2,64]{0,2,1:T(8,128)(2,1)S(1)}, bf16[4096,2,64]{0,2,1:T(8,128)(2,1)}, u32[]{:S(2)}) copy-start(bf16[4096,2,64]{0,2,1:T(8,128)(2,1)} %reshape_squeeze.31) | copy-start | bytes 3145732
Sparse Core Ops, SparseCore 0:
  74.6 56.1 all-gather.2
